TPU v7x, 128 devices: a whole 4x4x4 slice. The times are simulated.
128 devices in a mesh: ctx: 16 (over y, x), grp: 8 (over z, core).
Axes of the slice: x: 4, y: 4, z: 4, core: 2. Of those that a mesh axis runs over, the one named last changes fastest.
Arguments:
- residual: bfloat16 [8, 2048, 2880], P('grp', 'ctx'), may hold values from -3 to 3
- queries: bfloat16 [8, 2048, 2048], P('grp', 'ctx'), may hold values from -8 to 8
- stretch_kv: bfloat16 [8, 2048, 1024], P('grp', 'ctx'), may hold values from -8 to 8
- cache_kv: bfloat16 [8, 4096, 1024], P('grp', 'ctx'), may hold values from -6 to 6
- doc_lengths: int32 [8, 8], P('grp'), may hold values from 1 to 3072, 6144 in all within a row
- sinks: float32 [32], replicated, may hold values from 2 to 6
- out_proj: bfloat16 [2048, 2880], P('ctx'), may hold values from -0.75 to 0.75
- norm_gain: float32 [2880], replicated, may hold values from 0.1 to 1.9
- router: bfloat16 [2880, 64], replicated, may hold values from -0.109375 to 0.109375
- expert_ids: int32 [8, 2048, 4], P('grp', 'ctx'), may hold values from 0 to 63, all different within a row; in each aligned block of 128 rows (0 to 127, 128 to 255, ..., all dimensions but the last counted through in order) at most 10 rows name the same one
- expert_in: bfloat16 [128, 2880, 1536], P(('ctx', 'grp')), may hold values from -0.109375 to 0.109375
- expert_out: bfloat16 [128, 768, 2880], P(('ctx', 'grp')), may hold values from -0.15625 to 0.15625
Outputs:
- resid_mid: bfloat16 [8, 2048, 2880], P('grp', 'ctx')
- layer_out: bfloat16 [8, 2048, 2880], P('grp', 'ctx')
Inputs may be any that keep to these rules, and one draw needn't show every extreme that they name: `expert_ids`: in the rows of one device (aligned blocks of 128 tokens, sequence after sequence), each expert is named by at most 10 rows, and in some blocks one expert by exactly 10; a token's 4 experts differ. `doc_lengths`: A sequence's 8 lengths sum to 6144; the longest is exactly 3072.
All inputs are finite; a program needn't handle non-finite values.
Results may differ from a plain program's by a relative error of at most 0.015.
Values may be sent and summed in bfloat16 or wider, within the bound.
No kernel may reach another device: no remote copies, remote signals or barrier semaphores. Data moves between devices by JAX's collectives and lax.ppermute only.
A program may use at most 128 MiB of HBM per device.

v0:
```python
import math
import jax
import jax.numpy as jnp
from jax import lax
from jax.sharding import PartitionSpec as P

HEADS = 32
KVH = 8
HD = 64


def doc_index(positions, lengths):
    ends = jnp.cumsum(lengths)
    return jnp.sum((positions[:, None] >= ends[None, :]).astype(jnp.int32), axis=1)


def gated_act(pre, half_width):
    gate = pre[:, :half_width]
    upper = pre[:, half_width:]
    return ((upper + 1.0) * gate * jax.nn.sigmoid(1.702 * gate)).astype(jnp.bfloat16)


def body(
    residual,
    queries,
    stretch_kv,
    cache_kv,
    doc_lengths,
    sinks,
    out_proj,
    norm_gain,
    router,
    expert_ids,
    expert_in,
    expert_out,
):
    tokens = residual.shape[1]
    width = residual.shape[2]
    cache_rows = cache_kv.shape[1]
    kv_cols = stretch_kv.shape[2] // 2
    groups = HEADS // KVH
    ctx_count = lax.axis_size("ctx")
    ctx_here = lax.axis_index("ctx")
    stretch_base = cache_rows * ctx_count
    span = cache_rows + tokens
    query_pos = stretch_base + ctx_here * tokens + jnp.arange(tokens, dtype=jnp.int32)
    lengths = doc_lengths[0]
    query_doc = doc_index(query_pos, lengths)
    query_heads = queries[0].reshape(tokens, KVH, groups, HD)
    sink_grid = sinks.reshape(KVH, groups)
    local_kv = jnp.concatenate([cache_kv[0], stretch_kv[0]], axis=0)
    scale = 1.0 / math.sqrt(HD)

    def key_block(carry, keys_values, first):
        count = keys_values.shape[0]
        rows = first + jnp.arange(count, dtype=jnp.int32)
        source = rows // span
        offset = rows % span
        key_pos = jnp.where(
            offset < cache_rows,
            source * cache_rows + offset,
            stretch_base + source * tokens + offset - cache_rows,
        )
        key_doc = doc_index(key_pos, lengths)
        allowed = (key_pos[None, :] <= query_pos[:, None]) & (
            key_doc[None, :] == query_doc[:, None]
        )
        keys = keys_values[:, :kv_cols].reshape(count, KVH, HD)
        values = keys_values[:, kv_cols:].reshape(count, KVH, HD)
        top, total, numer = carry
        scores = (
            jnp.einsum("qkgd,skd->kgqs", query_heads, keys, preferred_element_type=jnp.float32)
            * scale
        )
        masked = jnp.where(allowed[None, None], scores, -jnp.inf)
        new_top = jnp.maximum(top, jnp.max(masked, axis=-1))
        weights = jnp.where(allowed[None, None], jnp.exp(scores - new_top[..., None]), 0.0)
        shrink = jnp.exp(top - new_top)
        total = total * shrink + jnp.sum(weights, axis=-1)
        numer = numer * shrink[..., None] + jnp.einsum(
            "kgqs,skd->kgqd",
            weights.astype(jnp.bfloat16),
            values,
            preferred_element_type=jnp.float32,
        )
        return (new_top, total, numer)

    start_top = jnp.broadcast_to(sink_grid[:, :, None], (KVH, groups, tokens))
    start_total = jnp.zeros((KVH, groups, tokens), jnp.float32)
    start_numer = jnp.zeros((KVH, groups, tokens, HD), jnp.float32)
    piece = lax.all_gather(local_kv, "ctx", axis=0, tiled=True)
    count = piece.shape[0]
    step_rows = math.gcd(count, 1024)

    def advance(index, state):
        first = index * step_rows
        part = lax.dynamic_slice_in_dim(piece, first, step_rows, 0)
        return key_block(state, part, first)

    top, total, numer = lax.fori_loop(
        0, count // step_rows, advance, (start_top, start_total, start_numer)
    )
    denom = total + jnp.exp(sink_grid[:, :, None] - top)
    attended = (
        jnp.transpose(numer / denom[..., None], (2, 0, 1, 3))
        .reshape(tokens, HEADS * HD)
        .astype(jnp.bfloat16)
    )
    projected = jnp.dot(
        attended,
        lax.all_gather(out_proj, "ctx", axis=0, tiled=True),
        preferred_element_type=jnp.float32,
    )
    mid = (residual[0].astype(jnp.float32) + projected).astype(jnp.bfloat16)
    mid_float = mid.astype(jnp.float32)
    normed = (
        mid_float
        * lax.rsqrt(jnp.mean(mid_float * mid_float, axis=-1, keepdims=True) + 1e-05)
        * norm_gain
    ).astype(jnp.bfloat16)
    logits = jnp.dot(normed, router, preferred_element_type=jnp.float32)
    experts = router.shape[1]
    chosen_ids = expert_ids[0]
    topk = chosen_ids.shape[1]
    picks = chosen_ids[:, :, None] == jnp.arange(experts, dtype=jnp.int32)[None, None, :]
    chosen = jnp.sum(jnp.where(picks, logits[:, None, :], 0.0), axis=-1)
    raised = jnp.exp(chosen)
    route_weights = raised / jnp.sum(raised, axis=-1, keepdims=True)
    capacity = 2 * ((5 * tokens * topk + 8 * experts - 1) // (8 * experts))
    flat_ids = chosen_ids.reshape(-1)
    pairs = flat_ids.shape[0]
    onehot = (flat_ids[:, None] == jnp.arange(experts, dtype=jnp.int32)[None, :]).astype(jnp.int32)
    slots = jnp.sum(onehot * (jnp.cumsum(onehot, axis=0) - 1), axis=1)
    dest = flat_ids * capacity + slots
    source_rows = jnp.arange(pairs, dtype=jnp.int32) // topk
    packed = jnp.zeros((experts * capacity, width), jnp.bfloat16).at[dest].set(normed[source_rows])
    packed = packed.reshape(experts, capacity, width)
    in_weights = expert_in[0]
    out_weights = expert_out[0]
    half_width = out_weights.shape[0]
    doubled = jnp.broadcast_to(packed[:, None], (experts, 2, capacity, width)).reshape(
        2 * experts, capacity, width
    )
    received = lax.all_to_all(doubled, ("ctx", "grp"), split_axis=0, concat_axis=0, tiled=True)
    flat_rows = received.reshape(-1, width)
    pre = jnp.dot(flat_rows, in_weights, preferred_element_type=jnp.float32)
    hidden = gated_act(pre, half_width)
    partial_out = jnp.dot(hidden, out_weights, preferred_element_type=jnp.float32).astype(
        jnp.bfloat16
    )
    partial_out = partial_out.reshape(received.shape)
    returned = lax.all_to_all(partial_out, ("ctx", "grp"), split_axis=0, concat_axis=0, tiled=True)
    pair_total = jnp.sum(returned.reshape(experts, 2, capacity, width).astype(jnp.float32), axis=1)
    expert_rows = pair_total.astype(jnp.bfloat16).reshape(experts * capacity, width)
    gathered = expert_rows[dest].astype(jnp.float32) * route_weights.reshape(-1)[:, None]
    mixture = jnp.sum(gathered.reshape(tokens, topk, width), axis=1)
    final = (mid_float + mixture).astype(jnp.bfloat16)
    return (mid[None], final[None])


def solution(mesh):
    return jax.shard_map(
        body,
        mesh=mesh,
        in_specs=(
            P("grp", "ctx", None),
            P("grp", "ctx", None),
            P("grp", "ctx", None),
            P("grp", "ctx", None),
            P("grp", None),
            P(),
            P("ctx", None),
            P(),
            P(),
            P("grp", "ctx", None),
            P(("ctx", "grp"), None, None),
            P(("ctx", "grp"), None, None),
        ),
        out_specs=(P("grp", "ctx", None), P("grp", "ctx", None)),
        check_vma=False,
    )
```

profile of v0, /device:TPU:66, one launch (start us, length us, event | category | flops | bytes accessed | tf_op | source)
XLA Modules:
  0.0 739.0 jit_solution(131095022201304216)
XLA Ops:
  7.3 1.3 copy.47
  8.6 1.1 copy.48
  9.7 1.0 pad_maximum_fusion
  12.6 1.2 reduce-window.20
  14.6 97.2 %all-gather.3.cloned.1.call-done = bf16[6144,1024]{0,1:T(8,128)(2,1)} async-done(((bf16[384,1024]{0,1:T(8,128)(2,1)}), bf16[6144,1024]{0,1:T(8,128)(2,1)}) %all-gather.3.cloned.1.call-update) | async-done | bytes 12582928 | tf_op jit(solution)/shard_map/all_gather | solution.py:91
  111.8 157.7 %while.20 = (s32[]{:T(128)}, f32[8,4,128]{2,1,0:T(4,128)S(1)}, f32[8,4,128]{2,1,0:T(4,128)S(1)}, f32[8,4,128,64]{2,3,1,0:T(8,128)S(1)}, s32[1,8]{1,0:T(1,128)S(1...) while((s32[]{:T(128)}, f32[8,4,128]{2,1,0:T(4,128)S(1)}, ...), condition=%wide.region_7.8_spmd.clone, body=%wide.region_3.7_spmd.clone.sunk | while | flops 1121116288 | bytes 60053240 | solution.py:100
  111.8 1.7 fusion.68
  114.0 7.1 fusion.69
  121.1 9.8 %fusion.70 = f32[8,4,128]{2,1,0:T(4,128)S(1)} fusion(f32[8,1024,128,4]{2,1,3,0:T(8,128)} %get-tuple-element.355, f32[8,4,128]{2,1,0:T(4,128)S(1)} %max.12, pred[128,1024]{0,1:T(8,128)(4,1)S(1)} %compare_and_fusion.2), kind=kLoop, calls=%fused_computation.10.clone.1 | loop fusion | flops 16773120 | bytes 16941056 | tf_op jit(solution)/shard_map/while/body/eval_jaxpr/reduce_sum | solution.py:79
  130.9 7.6 %fusion.72 = f32[8,4,128,64]{2,3,1,0:T(8,128)S(1)} fusion(bf16[1024,8,64,1]{0,2,3,1:T(8,128)(2,1)S(1)} %bitcast.98, f32[8,1024,128,4]{2,1,3,0:T(8,128)} %get-tuple-element.355, f32[8,4,128]{2,1,0:T(4,128)S(1)} %max.12, pred[128,1024]{0,1:T(8,128)(4,1)S(1)} %compare_and_fusion.2, f32[8,4,128,64]{2,3,1,0:T(8,128)S(1)} %get-tuple-element.376, ...), kind=kOutput, calls=%fused_computation.13.clone.1 | convolution fusion | flops 554434560 | bytes 20086784 | tf_op jit(solution)/shard_map/while/body/eval_jaxpr/kgqs,skd->kgqd/dot_general | solution.py:80
  138.6 1.8 fusion.68
  140.9 7.1 fusion.69
  147.9 9.1 %fusion.70 = f32[8,4,128]{2,1,0:T(4,128)S(1)} fusion(f32[8,1024,128,4]{2,1,3,0:T(8,128)} %get-tuple-element.355, f32[8,4,128]{2,1,0:T(4,128)S(1)} %max.12, pred[128,1024]{0,1:T(8,128)(4,1)S(1)} %compare_and_fusion.2), kind=kLoop, calls=%fused_computation.10.clone.1 | loop fusion | flops 16773120 | bytes 16941056 | tf_op jit(solution)/shard_map/while/body/eval_jaxpr/reduce_sum | solution.py:79
  157.1 7.8 %fusion.72 = f32[8,4,128,64]{2,3,1,0:T(8,128)S(1)} fusion(bf16[1024,8,64,1]{0,2,3,1:T(8,128)(2,1)S(1)} %bitcast.98, f32[8,1024,128,4]{2,1,3,0:T(8,128)} %get-tuple-element.355, f32[8,4,128]{2,1,0:T(4,128)S(1)} %max.12, pred[128,1024]{0,1:T(8,128)(4,1)S(1)} %compare_and_fusion.2, f32[8,4,128,64]{2,3,1,0:T(8,128)S(1)} %get-tuple-element.376, ...), kind=kOutput, calls=%fused_computation.13.clone.1 | convolution fusion | flops 554434560 | bytes 20086784 | tf_op jit(solution)/shard_map/while/body/eval_jaxpr/kgqs,skd->kgqd/dot_general | solution.py:80
  164.9 1.7 fusion.68
  167.1 7.2 fusion.69
  174.3 9.8 %fusion.70 = f32[8,4,128]{2,1,0:T(4,128)S(1)} fusion(f32[8,1024,128,4]{2,1,3,0:T(8,128)} %get-tuple-element.355, f32[8,4,128]{2,1,0:T(4,128)S(1)} %max.12, pred[128,1024]{0,1:T(8,128)(4,1)S(1)} %compare_and_fusion.2), kind=kLoop, calls=%fused_computation.10.clone.1 | loop fusion | flops 16773120 | bytes 16941056 | tf_op jit(solution)/shard_map/while/body/eval_jaxpr/reduce_sum | solution.py:79
  184.2 7.4 %fusion.72 = f32[8,4,128,64]{2,3,1,0:T(8,128)S(1)} fusion(bf16[1024,8,64,1]{0,2,3,1:T(8,128)(2,1)S(1)} %bitcast.98, f32[8,1024,128,4]{2,1,3,0:T(8,128)} %get-tuple-element.355, f32[8,4,128]{2,1,0:T(4,128)S(1)} %max.12, pred[128,1024]{0,1:T(8,128)(4,1)S(1)} %compare_and_fusion.2, f32[8,4,128,64]{2,3,1,0:T(8,128)S(1)} %get-tuple-element.376, ...), kind=kOutput, calls=%fused_computation.13.clone.1 | convolution fusion | flops 554434560 | bytes 20086784 | tf_op jit(solution)/shard_map/while/body/eval_jaxpr/kgqs,skd->kgqd/dot_general | solution.py:80
  191.6 1.8 fusion.68
  193.9 7.2 fusion.69
  201.1 9.1 %fusion.70 = f32[8,4,128]{2,1,0:T(4,128)S(1)} fusion(f32[8,1024,128,4]{2,1,3,0:T(8,128)} %get-tuple-element.355, f32[8,4,128]{2,1,0:T(4,128)S(1)} %max.12, pred[128,1024]{0,1:T(8,128)(4,1)S(1)} %compare_and_fusion.2), kind=kLoop, calls=%fused_computation.10.clone.1 | loop fusion | flops 16773120 | bytes 16941056 | tf_op jit(solution)/shard_map/while/body/eval_jaxpr/reduce_sum | solution.py:79
  210.2 7.4 %fusion.72 = f32[8,4,128,64]{2,3,1,0:T(8,128)S(1)} fusion(bf16[1024,8,64,1]{0,2,3,1:T(8,128)(2,1)S(1)} %bitcast.98, f32[8,1024,128,4]{2,1,3,0:T(8,128)} %get-tuple-element.355, f32[8,4,128]{2,1,0:T(4,128)S(1)} %max.12, pred[128,1024]{0,1:T(8,128)(4,1)S(1)} %compare_and_fusion.2, f32[8,4,128,64]{2,3,1,0:T(8,128)S(1)} %get-tuple-element.376, ...), kind=kOutput, calls=%fused_computation.13.clone.1 | convolution fusion | flops 554434560 | bytes 20086784 | tf_op jit(solution)/shard_map/while/body/eval_jaxpr/kgqs,skd->kgqd/dot_general | solution.py:80
  217.7 1.7 fusion.68
  219.9 7.1 fusion.69
  226.9 9.1 %fusion.70 = f32[8,4,128]{2,1,0:T(4,128)S(1)} fusion(f32[8,1024,128,4]{2,1,3,0:T(8,128)} %get-tuple-element.355, f32[8,4,128]{2,1,0:T(4,128)S(1)} %max.12, pred[128,1024]{0,1:T(8,128)(4,1)S(1)} %compare_and_fusion.2), kind=kLoop, calls=%fused_computation.10.clone.1 | loop fusion | flops 16773120 | bytes 16941056 | tf_op jit(solution)/shard_map/while/body/eval_jaxpr/reduce_sum | solution.py:79
  236.1 7.4 %fusion.72 = f32[8,4,128,64]{2,3,1,0:T(8,128)S(1)} fusion(bf16[1024,8,64,1]{0,2,3,1:T(8,128)(2,1)S(1)} %bitcast.98, f32[8,1024,128,4]{2,1,3,0:T(8,128)} %get-tuple-element.355, f32[8,4,128]{2,1,0:T(4,128)S(1)} %max.12, pred[128,1024]{0,1:T(8,128)(4,1)S(1)} %compare_and_fusion.2, f32[8,4,128,64]{2,3,1,0:T(8,128)S(1)} %get-tuple-element.376, ...), kind=kOutput, calls=%fused_computation.13.clone.1 | convolution fusion | flops 554434560 | bytes 20086784 | tf_op jit(solution)/shard_map/while/body/eval_jaxpr/kgqs,skd->kgqd/dot_general | solution.py:80
  243.5 1.7 fusion.68
  245.7 7.1 fusion.69
  252.8 9.1 %fusion.70 = f32[8,4,128]{2,1,0:T(4,128)S(1)} fusion(f32[8,1024,128,4]{2,1,3,0:T(8,128)} %get-tuple-element.355, f32[8,4,128]{2,1,0:T(4,128)S(1)} %max.12, pred[128,1024]{0,1:T(8,128)(4,1)S(1)} %compare_and_fusion.2), kind=kLoop, calls=%fused_computation.10.clone.1 | loop fusion | flops 16773120 | bytes 16941056 | tf_op jit(solution)/shard_map/while/body/eval_jaxpr/reduce_sum | solution.py:79
  261.9 7.4 %fusion.72 = f32[8,4,128,64]{2,3,1,0:T(8,128)S(1)} fusion(bf16[1024,8,64,1]{0,2,3,1:T(8,128)(2,1)S(1)} %bitcast.98, f32[8,1024,128,4]{2,1,3,0:T(8,128)} %get-tuple-element.355, f32[8,4,128]{2,1,0:T(4,128)S(1)} %max.12, pred[128,1024]{0,1:T(8,128)(4,1)S(1)} %compare_and_fusion.2, f32[8,4,128,64]{2,3,1,0:T(8,128)S(1)} %get-tuple-element.376, ...), kind=kOutput, calls=%fused_computation.13.clone.1 | convolution fusion | flops 554434560 | bytes 20086784 | tf_op jit(solution)/shard_map/while/body/eval_jaxpr/kgqs,skd->kgqd/dot_general | solution.py:80
  269.7 7.7 %fusion.35 = (f32[128]{0:T(128)S(1)}, bf16[128,2880]{0,1:T(8,128)(2,1)S(1)}) fusion(bf16[2048,2880]{0,1:T(8,128)(2,1)} %all-gather.5.cloned.1.call-done, bf16[128,2048]{0,1:T(8,128)(2,1)S(1)} %bitcast.102, bf16[1,128,2880]{1,2,0:T(8,128)(2,1)} %param.14), kind=kOutput, calls=%fused_computation.55 | convolution fusion | flops 1512161152 | bytes 13795840 | tf_op jit(solution)/shard_map/dot_general | solution.py:109
  279.1 16.4 %scatter_custom_fusion = bf16[640,2880]{1,0:T(8,128)(2,1)} fusion(s32[512]{0:T(512)S(1)} %bitcast.106, bf16[128,2880]{1,0:T(8,128)(2,1)S(1)} %copy.54, s32[1024]{0:T(1024)S(1)} %pad_clamp_fusion.1, bf16[]{:T(256)} %constant.176.clone.1), kind=kCustom, calls=%fused_computation.47 | custom fusion | bytes 3686402 | tf_op jit(solution)/shard_map/scatter | solution.py:136
  295.6 7.3 broadcast_in_dim.138
  302.8 4.5 broadcast_in_dim.139
  307.4 142.9 %all_to_all.10 = bf16[128,10,2880]{2,1,0:T(8,128)(2,1)} all-to-all(bf16[128,10,2880]{2,1,0:T(8,128)(2,1)S(1)} %bitcast.97), channel_id=1, replica_groups=mesh['ctx'=16,'grp'=8] {'ctx','grp'}, dimensions={0} | all-to-all | bytes 14745600 | tf_op jit(solution)/shard_map/all_to_all | solution.py:144
  450.2 14.4 %reshape.320 = bf16[1280,2880]{1,0:T(8,128)(2,1)} reshape(bf16[128,10,2880]{2,1,0:T(8,128)(2,1)} %all_to_all.10) | data formatting | bytes 14745600 | tf_op jit(solution)/shard_map/reshape | solution.py:145
  464.6 17.2 %fusion.22 = f32[1280,1536]{1,0:T(8,128)S(1)} fusion(bf16[1280,2880]{1,0:T(8,128)(2,1)} %reshape.320, bf16[1,2880,1536]{2,1,0:T(8,128)(2,1)} %param.24), kind=kOutput, calls=%fused_computation.37 | convolution fusion | flops 11324620800 | bytes 24084480 | tf_op jit(solution)/shard_map/dot_general | solution.py:146
  481.9 11.8 %convolution_convert_fusion = bf16[1280,2880]{0,1:T(8,128)(2,1)} fusion(bf16[1,768,2880]{1,2,0:T(8,128)(2,1)} %param.25, f32[1280,1536]{1,0:T(8,128)S(1)} %fusion.22), kind=kOutput, calls=%fused_computation.36 | convolution fusion | flops 5673861120 | bytes 19660800 | tf_op jit(solution)/shard_map/dot_general | solution.py:148
  493.6 10.4 %copy.55 = bf16[1280,2880]{1,0:T(8,128)(2,1)} copy(bf16[1280,2880]{0,1:T(8,128)(2,1)} %convolution_convert_fusion) | data formatting | bytes 14745600 | tf_op jit(solution)/shard_map/convert_element_type | solution.py:148
  504.1 13.4 %reshape.321 = bf16[128,10,2880]{2,1,0:T(8,128)(2,1)} reshape(bf16[1280,2880]{1,0:T(8,128)(2,1)} %copy.55) | data formatting | bytes 14745600 | tf_op jit(solution)/shard_map/reshape | solution.py:151
  517.5 12.0 %all-to-all-start.1 = ((bf16[128,10,2880]{2,1,0:T(8,128)(2,1)}), bf16[128,10,2880]{2,1,0:T(8,128)(2,1)}, u32[]{:S(2)}, u32[]{:S(2)}) async-start(bf16[128,10,2880]{2,1,0:T(8,128)(2,1)} %reshape.321), calls=%async_computation.1 | async-start | bytes 24117248 | tf_op jit(solution)/shard_map/all_to_all | solution.py:152
  530.0 157.7 %all-to-all-done.1 = bf16[128,10,2880]{2,1,0:T(8,128)(2,1)} async-done(((bf16[128,10,2880]{2,1,0:T(8,128)(2,1)}), bf16[128,10,2880]{2,1,0:T(8,128)(2,1)}, u32[]{:S(2)}, u32[]{:S(2)}) %all-to-all-start.1) | async-done | bytes 7372832 | tf_op jit(solution)/shard_map/all_to_all | solution.py:152
  687.7 14.7 %bitcast_reduce_fusion = bf16[64,10,2880]{2,1,0:T(8,128)(2,1)} fusion(bf16[128,10,2880]{2,1,0:T(8,128)(2,1)} %all-to-all-done.1), kind=kLoop, calls=%fused_computation.35 | loop fusion | flops 1843200 | bytes 11059200 | tf_op jit(solution)/shard_map/reduce_sum | solution.py:153
  702.4 7.8 %reshape.323 = bf16[640,2880]{1,0:T(8,128)(2,1)} reshape(bf16[64,10,2880]{2,1,0:T(8,128)(2,1)} %bitcast_reduce_fusion) | data formatting | bytes 7372800 | tf_op jit(solution)/shard_map/reshape | solution.py:154
  710.2 8.4 %gather_fusion = bf16[512,2880]{1,0:T(8,128)(2,1)S(1)} fusion(bf16[640,2880]{1,0:T(8,128)(2,1)} %reshape.323, s32[1024]{0:T(1024)S(1)} %pad_clamp_fusion), kind=kCustom, calls=%fused_computation.1 | custom fusion | bytes 5900288 | tf_op jit(solution)/shard_map/gather | solution.py:155
  718.5 3.8 reshape.325
  722.3 7.0 multiply_reduce_fusion
  729.8 2.1 fusion.39
  (98 shorter events, 8.3 us)
Async XLA Ops:
  7.2 522.4 %copy-start = (bf16[2880,64]{0,1:T(8,128)(2,1)S(1)}, bf16[2880,64]{0,1:T(8,128)(2,1)}, u32[]{:S(2)}) copy-start(bf16[2880,64]{0,1:T(8,128)(2,1)} %param.22) | copy-start | bytes 1105924
  7.2 4.3 copy-start.3
  7.2 4.7 copy-start.6
  7.2 4.8 copy-start.7
  7.2 5.1 copy-start.2
  7.2 104.5 %all-gather.3.cloned.1.call-start = ((), (), s32[]{:S(2)}) async-start(), calls=%async_computation.2 | async-start | bytes 13369344 | tf_op jit(solution)/shard_map/all_gather | solution.py:91
  10.7 259.0 %all-gather.5.cloned.1.call-start = ((), (), s32[]{:S(2)}) async-start(), calls=%async_computation.3 | async-start | bytes 12533760 | tf_op jit(solution)/shard_map/all_gather | solution.py:111
  269.7 8.6 %copy-start.5 = (f32[2880]{0:T(1024)S(1)}, f32[2880]{0:T(1024)}, u32[]{:S(2)}) copy-start(f32[2880]{0:T(1024)} %param.21) | copy-start | bytes 34564
  277.5 0.9 copy-start.1
  517.5 12.3 %copy-start.4 = (s32[1,128,4]{1,2,0:T(4,128)S(1)}, s32[1,128,4]{1,2,0:T(4,128)}, u32[]{:S(2)}) copy-start(s32[1,128,4]{1,2,0:T(4,128)} %param.23) | copy-start | bytes 6148
  517.5 170.2 %all-to-all-start.1 = ((bf16[128,10,2880]{2,1,0:T(8,128)(2,1)}), bf16[128,10,2880]{2,1,0:T(8,128)(2,1)}, u32[]{:S(2)}, u32[]{:S(2)}) async-start(bf16[128,10,2880]{2,1,0:T(8,128)(2,1)} %reshape.321), calls=%async_computation.1 | async-start | bytes 24117248 | tf_op jit(solution)/shard_map/all_to_all | solution.py:152
Sparse Core Ops, SparseCore 0:
  10.8 100.8 all-gather.2
  113.8 94.9 all-gather.4
where the time goes:
time: 747 us; the launch traced here: 739 us
  waiting for transfers between devices  256 us (34%)
  blocking collectives  143 us (19%)
  matrix products  125 us (17%)
  local copies, waits for them, and re-layouts  102 us (14%)
  other arithmetic  86.3 us (12%)
  between operations  14.6 us (2%)
  starting transfers between devices  12.1 us (2%)
    all_to_all x1, waiting for transfers between devices, body(): lax.all_to_all(partial_out, ('ctx', 'grp'), split_axis=0, concat_axis=0,...  158 us
    all_to_all x1, blocking collectives, body(): lax.all_to_all(doubled, ('ctx', 'grp'), split_axis=0, concat_axis=0, tile...  143 us
    all_gather x1, waiting for transfers between devices, body(): piece = lax.all_gather(local_kv, 'ctx', axis=0, tiled=True)  97.2 us
    reduce_sum x6, other arithmetic, key_block(): total = total * shrink + jnp.sum(weights, axis=-1)  56 us
    dot_general x6, matrix products, key_block(): jnp.einsum('kgqs,skd->kgqd', weights.astype(jnp.bfloat16), values, prefer...  45 us
    dot_general x6, matrix products, key_block(): jnp.einsum('qkgd,skd->kgqs', query_heads, keys, preferred_element_type=jn...  42.7 us
    dot_general x1, matrix products, body(): pre = jnp.dot(flat_rows, in_weights, preferred_element_type=jnp.float32)  17.2 us
    scatter x1, local copies, waits for them, and re-layouts, body(): jnp.zeros((experts * capacity, width), jnp.bfloat16).at[dest]  16.4 us
  transfers between devices with their start and end apart: 3, of which 2 were waited for; matrix products, arithmetic and copies ran while one was open for 22% of the time, Pallas kernels for 0%

commit v1 on v0

--- a/solution.py
+++ b/solution.py
@@ -7,6 +7,25 @@
 HEADS = 32
 KVH = 8
 HD = 64
+
+
+def wrap_types(frame, chip_axis="ctx"):
+    lanes = lax.axis_size(chip_axis)
+    nodes = [(dev_j, (dev_j + 1) % lanes) for dev_j in range(lanes)]
+    row_list = [(dev_j, (dev_j - 1) % lanes) for dev_j in range(lanes)]
+    high, p_next = ([frame], [frame])
+    for _ in range(lanes // 2):
+        high.append(lax.ppermute(high[-1], chip_axis, nodes))
+    u = 0
+    while u < (lanes - 1) // 2:
+        p_next.append(lax.ppermute(p_next[-1], axis_name=chip_axis, perm=row_list))
+        u += 1
+    tile_out = jnp.roll(
+        jnp.concatenate([*high[::-1], *p_next[1:]], 0),
+        (lax.axis_index(chip_axis) - lanes // 2) * frame.shape[0],
+        0,
+    )
+    return tile_out
 
 
 def doc_index(positions, lengths):
@@ -88,7 +107,7 @@
     start_top = jnp.broadcast_to(sink_grid[:, :, None], (KVH, groups, tokens))
     start_total = jnp.zeros((KVH, groups, tokens), jnp.float32)
     start_numer = jnp.zeros((KVH, groups, tokens, HD), jnp.float32)
-    piece = lax.all_gather(local_kv, "ctx", axis=0, tiled=True)
+    piece = wrap_types(local_kv)
     count = piece.shape[0]
     step_rows = math.gcd(count, 1024)
 

time: 747 us -> 844 us (1.13)
  starting transfers between devices: 12.1 us -> 55.4 us
  local copies, waits for them, and re-layouts: 102 us -> 137 us
  waiting for transfers between devices: 256 us -> 272 us
    ppermute x0 -> x15, waiting for transfers between devices: none -> 114 us  [the longest x8 102 us: wrap_types(): high.append(lax.ppermute(high[-1], chip_axis, nodes))]
    all_gather x1 -> x0, waiting for transfers between devices: 97.2 us -> none  [body(): piece = lax.all_gather(local_kv, 'ctx', axis=0, tiled=True)]
    ppermute x0 -> x15, starting transfers between devices: none -> 43.3 us  [the longest x7 40.2 us: wrap_types(): p_next.append(lax.ppermute(p_next[-1], axis_name=chip_axis, perm=row_list))]
    unnamed x20 -> x71, local copies, waits for them, and re-layouts: 3.72 us -> 26.9 us
    dynamic_slice x0 -> x1, local copies, waits for them, and re-layouts: none -> 11 us  [wrap_types(): jnp.roll(jnp.concatenate([*high[::-1], *p_next[1:]], 0), (lax.axis_index(...]
  transfers between devices with their start and end apart: 3 -> 17, of which waited for: 2 -> 10; matrix products, arithmetic and copies ran while one was open for 22% -> 24% of each run, Pallas kernels for 0% -> 0%
where the time goes in v1:
time: 844 us; the launch traced here: 835 us
  waiting for transfers between devices  272 us (32%)
  blocking collectives  144 us (17%)
  local copies, waits for them, and re-layouts  137 us (16%)
  matrix products  124 us (15%)
  other arithmetic  86.6 us (10%)
  starting transfers between devices  55.4 us (7%)
  between operations  15.3 us (2%)
    all_to_all x1, waiting for transfers between devices, body(): lax.all_to_all(partial_out, ('ctx', 'grp'), split_axis=0, concat_axis=0,...  158 us
    all_to_all x1, blocking collectives, body(): lax.all_to_all(doubled, ('ctx', 'grp'), split_axis=0, concat_axis=0, tile...  144 us
    ppermute x8, waiting for transfers between devices, wrap_types(): high.append(lax.ppermute(high[-1], chip_axis, nodes))  102 us
    reduce_sum x6, other arithmetic, key_block(): total = total * shrink + jnp.sum(weights, axis=-1)  55.2 us
    dot_general x6, matrix products, key_block(): jnp.einsum('kgqs,skd->kgqd', weights.astype(jnp.bfloat16), values, prefer...  44.4 us
    dot_general x6, matrix products, key_block(): jnp.einsum('qkgd,skd->kgqs', query_heads, keys, preferred_element_type=jn...  42.7 us
    ppermute x7, starting transfers between devices, wrap_types(): p_next.append(lax.ppermute(p_next[-1], axis_name=chip_axis, perm=row_list))  40.2 us
    unnamed x71, local copies, waits for them, and re-layouts  26.9 us
  transfers between devices with their start and end apart: 17, of which 10 were waited for; matrix products, arithmetic and copies ran while one was open for 24% of the time, Pallas kernels for 0%

profile of v1, /device:TPU:66, one launch (start us, length us, event | category | flops | bytes accessed | tf_op | source)
XLA Modules:
  0.0 835.3 jit_solution(15397931724016249860)
XLA Ops:
  11.3 17.8 %collective-permute-done = bf16[384,1024]{0,1:T(8,128)(2,1)S(1)} collective-permute-done((bf16[384,1024]{0,1:T(8,128)(2,1)S(1)}, bf16[384,1024]{0,1:T(8,128)(2,1)S(1)}, u32[]{:S(2)}, u32[]{:S(2)}) %collective-permute-start) | collective-permute-done | bytes 786464 | tf_op jit(solution)/shard_map/ppermute | solution.py:18
  33.1 16.8 %collective-permute-done.1 = bf16[384,1024]{0,1:T(8,128)(2,1)S(1)} collective-permute-done((bf16[384,1024]{0,1:T(8,128)(2,1)S(1)}, bf16[384,1024]{0,1:T(8,128)(2,1)S(1)}, u32[]{:S(2)}, u32[]{:S(2)}) %collective-permute-start.1) | collective-permute-done | bytes 786464 | tf_op jit(solution)/shard_map/ppermute | solution.py:18
  49.9 5.1 collective-permute-start.9
  55.1 15.8 %collective-permute-done.2 = bf16[384,1024]{0,1:T(8,128)(2,1)S(1)} collective-permute-done((bf16[384,1024]{0,1:T(8,128)(2,1)S(1)}, bf16[384,1024]{0,1:T(8,128)(2,1)S(1)}, u32[]{:S(2)}, u32[]{:S(2)}) %collective-permute-start.2) | collective-permute-done | bytes 786464 | tf_op jit(solution)/shard_map/ppermute | solution.py:18
  70.9 5.1 collective-permute-start.10
  76.1 14.9 %collective-permute-done.3 = bf16[384,1024]{0,1:T(8,128)(2,1)S(1)} collective-permute-done((bf16[384,1024]{0,1:T(8,128)(2,1)S(1)}, bf16[384,1024]{0,1:T(8,128)(2,1)S(1)}, u32[]{:S(2)}, u32[]{:S(2)}) %collective-permute-start.3) | collective-permute-done | bytes 786464 | tf_op jit(solution)/shard_map/ppermute | solution.py:18
  91.0 5.1 collective-permute-start.11
  96.1 14.0 %collective-permute-done.4 = bf16[384,1024]{0,1:T(8,128)(2,1)S(1)} collective-permute-done((bf16[384,1024]{0,1:T(8,128)(2,1)S(1)}, bf16[384,1024]{0,1:T(8,128)(2,1)S(1)}, u32[]{:S(2)}, u32[]{:S(2)}) %collective-permute-start.4) | collective-permute-done | bytes 786464 | tf_op jit(solution)/shard_map/ppermute | solution.py:18
  110.1 5.1 collective-permute-start.12
  115.3 13.2 %collective-permute-done.5 = bf16[384,1024]{0,1:T(8,128)(2,1)} collective-permute-done((bf16[384,1024]{0,1:T(8,128)(2,1)S(1)}, bf16[384,1024]{0,1:T(8,128)(2,1)}, u32[]{:S(2)}, u32[]{:S(2)}) %collective-permute-start.5) | collective-permute-done | bytes 786464 | tf_op jit(solution)/shard_map/ppermute | solution.py:18
  140.8 5.3 collective-permute-done.6
  146.4 12.4 %collective-permute-done.13 = bf16[384,1024]{0,1:T(8,128)(2,1)S(1)} collective-permute-done((bf16[384,1024]{0,1:T(8,128)(2,1)}, bf16[384,1024]{0,1:T(8,128)(2,1)S(1)}, u32[]{:S(2)}, u32[]{:S(2)}) %collective-permute-start.13) | collective-permute-done | bytes 786464 | tf_op jit(solution)/shard_map/ppermute | solution.py:21
  158.7 12.0 %collective-permute-start.14 = (bf16[384,1024]{0,1:T(8,128)(2,1)S(1)}, bf16[384,1024]{0,1:T(8,128)(2,1)S(1)}, u32[]{:S(2)}, u32[]{:S(2)}) collective-permute-start(bf16[384,1024]{0,1:T(8,128)(2,1)S(1)} %collective-permute-done.13), channel_id=1, source_target_pairs={{0,120},{8,0},{16,8},{24,16},{32,24},{40,32},{48,40},{56,48},{64,5... | collective-permute-start | bytes 2359304 | tf_op jit(solution)/shard_map/ppermute | solution.py:21
  196.7 11.0 %constant_dynamic-slice_fusion.1 = bf16[6144,1024]{0,1:T(8,128)(2,1)} fusion(bf16[12288,1024]{0,1:T(8,128)(2,1)S(1)} %constant_dynamic-update-slice_fusion, s32[]{:T(128)S(6)} %select_n.162), kind=kLoop, calls=%fused_computation.121 | loop fusion | bytes 25165828 | tf_op jit(solution)/shard_map/jit(_roll_dynamic)/dynamic_slice | solution.py:23
  207.8 156.5 %while.20 = (s32[]{:T(128)}, f32[8,4,128]{2,1,0:T(4,128)S(1)}, f32[8,4,128]{2,1,0:T(4,128)S(1)}, f32[8,4,128,64]{2,3,1,0:T(8,128)S(1)}, s32[1,8]{1,0:T(1,128)S(1...) while((s32[]{:T(128)}, f32[8,4,128]{2,1,0:T(4,128)S(1)}, ...), condition=%wide.region_7.8_spmd.clone, body=%wide.region_3.7_spmd.clone.sunk | while | flops 1121116288 | bytes 60053240 | solution.py:119
  210.0 7.2 fusion.69
  217.2 9.8 %fusion.70 = f32[8,4,128]{2,1,0:T(4,128)S(1)} fusion(f32[8,1024,128,4]{2,1,3,0:T(8,128)} %get-tuple-element.355, f32[8,4,128]{2,1,0:T(4,128)S(1)} %max.12, pred[128,1024]{0,1:T(8,128)(4,1)S(1)} %compare_and_fusion.2), kind=kLoop, calls=%fused_computation.10.clone.1 | loop fusion | flops 16773120 | bytes 16941056 | tf_op jit(solution)/shard_map/while/body/eval_jaxpr/reduce_sum | solution.py:98
  227.0 7.4 fusion.72
  236.7 7.3 fusion.69
  244.0 9.1 %fusion.70 = f32[8,4,128]{2,1,0:T(4,128)S(1)} fusion(f32[8,1024,128,4]{2,1,3,0:T(8,128)} %get-tuple-element.355, f32[8,4,128]{2,1,0:T(4,128)S(1)} %max.12, pred[128,1024]{0,1:T(8,128)(4,1)S(1)} %compare_and_fusion.2), kind=kLoop, calls=%fused_computation.10.clone.1 | loop fusion | flops 16773120 | bytes 16941056 | tf_op jit(solution)/shard_map/while/body/eval_jaxpr/reduce_sum | solution.py:98
  253.2 7.4 fusion.72
  262.8 7.1 fusion.69
  269.8 9.1 %fusion.70 = f32[8,4,128]{2,1,0:T(4,128)S(1)} fusion(f32[8,1024,128,4]{2,1,3,0:T(8,128)} %get-tuple-element.355, f32[8,4,128]{2,1,0:T(4,128)S(1)} %max.12, pred[128,1024]{0,1:T(8,128)(4,1)S(1)} %compare_and_fusion.2), kind=kLoop, calls=%fused_computation.10.clone.1 | loop fusion | flops 16773120 | bytes 16941056 | tf_op jit(solution)/shard_map/while/body/eval_jaxpr/reduce_sum | solution.py:98
  279.0 7.4 fusion.72
  288.6 7.1 fusion.69
  295.7 9.1 %fusion.70 = f32[8,4,128]{2,1,0:T(4,128)S(1)} fusion(f32[8,1024,128,4]{2,1,3,0:T(8,128)} %get-tuple-element.355, f32[8,4,128]{2,1,0:T(4,128)S(1)} %max.12, pred[128,1024]{0,1:T(8,128)(4,1)S(1)} %compare_and_fusion.2), kind=kLoop, calls=%fused_computation.10.clone.1 | loop fusion | flops 16773120 | bytes 16941056 | tf_op jit(solution)/shard_map/while/body/eval_jaxpr/reduce_sum | solution.py:98
  304.8 7.4 fusion.72
  314.4 7.1 fusion.69
  321.5 9.1 %fusion.70 = f32[8,4,128]{2,1,0:T(4,128)S(1)} fusion(f32[8,1024,128,4]{2,1,3,0:T(8,128)} %get-tuple-element.355, f32[8,4,128]{2,1,0:T(4,128)S(1)} %max.12, pred[128,1024]{0,1:T(8,128)(4,1)S(1)} %compare_and_fusion.2), kind=kLoop, calls=%fused_computation.10.clone.1 | loop fusion | flops 16773120 | bytes 16941056 | tf_op jit(solution)/shard_map/while/body/eval_jaxpr/reduce_sum | solution.py:98
  330.6 7.4 fusion.72
  340.2 7.1 fusion.69
  347.3 9.1 %fusion.70 = f32[8,4,128]{2,1,0:T(4,128)S(1)} fusion(f32[8,1024,128,4]{2,1,3,0:T(8,128)} %get-tuple-element.355, f32[8,4,128]{2,1,0:T(4,128)S(1)} %max.12, pred[128,1024]{0,1:T(8,128)(4,1)S(1)} %compare_and_fusion.2), kind=kLoop, calls=%fused_computation.10.clone.1 | loop fusion | flops 16773120 | bytes 16941056 | tf_op jit(solution)/shard_map/while/body/eval_jaxpr/reduce_sum | solution.py:98
  356.4 7.4 fusion.72
  364.6 7.7 fusion.35
  374.0 16.4 %scatter_custom_fusion = bf16[640,2880]{1,0:T(8,128)(2,1)} fusion(s32[512]{0:T(512)S(1)} %bitcast.110, bf16[128,2880]{1,0:T(8,128)(2,1)S(1)} %copy.54, s32[1024]{0:T(1024)S(1)} %pad_clamp_fusion.1, bf16[]{:T(256)} %constant.199.clone.1), kind=kCustom, calls=%fused_computation.47 | custom fusion | bytes 3686402 | tf_op jit(solution)/shard_map/scatter | solution.py:155
  390.4 7.3 broadcast_in_dim.138
  402.2 144.0 %all_to_all.10 = bf16[128,10,2880]{2,1,0:T(8,128)(2,1)} all-to-all(bf16[128,10,2880]{2,1,0:T(8,128)(2,1)S(1)} %bitcast.101), channel_id=1, replica_groups=mesh['ctx'=16,'grp'=8] {'ctx','grp'}, dimensions={0} | all-to-all | bytes 14745600 | tf_op jit(solution)/shard_map/all_to_all | solution.py:163
  546.2 14.4 %reshape.320 = bf16[1280,2880]{1,0:T(8,128)(2,1)} reshape(bf16[128,10,2880]{2,1,0:T(8,128)(2,1)} %all_to_all.10) | data formatting | bytes 14745600 | tf_op jit(solution)/shard_map/reshape | solution.py:164
  560.5 17.2 %fusion.22 = f32[1280,1536]{1,0:T(8,128)S(1)} fusion(bf16[1280,2880]{1,0:T(8,128)(2,1)} %reshape.320, bf16[1,2880,1536]{2,1,0:T(8,128)(2,1)} %param.24), kind=kOutput, calls=%fused_computation.37 | convolution fusion | flops 11324620800 | bytes 24084480 | tf_op jit(solution)/shard_map/dot_general | solution.py:165
  577.8 11.8 %convolution_convert_fusion = bf16[1280,2880]{0,1:T(8,128)(2,1)} fusion(bf16[1,768,2880]{1,2,0:T(8,128)(2,1)} %param.25, f32[1280,1536]{1,0:T(8,128)S(1)} %fusion.22), kind=kOutput, calls=%fused_computation.36 | convolution fusion | flops 5673861120 | bytes 19660800 | tf_op jit(solution)/shard_map/dot_general | solution.py:167
  589.6 10.4 %copy.55 = bf16[1280,2880]{1,0:T(8,128)(2,1)} copy(bf16[1280,2880]{0,1:T(8,128)(2,1)} %convolution_convert_fusion) | data formatting | bytes 14745600 | tf_op jit(solution)/shard_map/convert_element_type | solution.py:167
  600.0 13.4 %reshape.321 = bf16[128,10,2880]{2,1,0:T(8,128)(2,1)} reshape(bf16[1280,2880]{1,0:T(8,128)(2,1)} %copy.55) | data formatting | bytes 14745600 | tf_op jit(solution)/shard_map/reshape | solution.py:170
  613.4 12.1 %all-to-all-start.1 = ((bf16[128,10,2880]{2,1,0:T(8,128)(2,1)}), bf16[128,10,2880]{2,1,0:T(8,128)(2,1)}, u32[]{:S(2)}, u32[]{:S(2)}) async-start(bf16[128,10,2880]{2,1,0:T(8,128)(2,1)} %reshape.321), calls=%async_computation.1 | async-start | bytes 24117248 | tf_op jit(solution)/shard_map/all_to_all | solution.py:171
  626.0 157.7 %all-to-all-done.1 = bf16[128,10,2880]{2,1,0:T(8,128)(2,1)} async-done(((bf16[128,10,2880]{2,1,0:T(8,128)(2,1)}), bf16[128,10,2880]{2,1,0:T(8,128)(2,1)}, u32[]{:S(2)}, u32[]{:S(2)}) %all-to-all-start.1) | async-done | bytes 7372832 | tf_op jit(solution)/shard_map/all_to_all | solution.py:171
  783.7 14.7 %bitcast_reduce_fusion = bf16[64,10,2880]{2,1,0:T(8,128)(2,1)} fusion(bf16[128,10,2880]{2,1,0:T(8,128)(2,1)} %all-to-all-done.1), kind=kLoop, calls=%fused_computation.35 | loop fusion | flops 1843200 | bytes 11059200 | tf_op jit(solution)/shard_map/reduce_sum | solution.py:172
  798.4 7.8 reshape.323
  806.2 8.4 %gather_fusion = bf16[512,2880]{1,0:T(8,128)(2,1)S(1)} fusion(bf16[640,2880]{1,0:T(8,128)(2,1)} %reshape.323, s32[1024]{0:T(1024)S(1)} %pad_clamp_fusion), kind=kCustom, calls=%fused_computation.1 | custom fusion | bytes 5900288 | tf_op jit(solution)/shard_map/gather | solution.py:174
  818.4 7.0 multiply_reduce_fusion
  (178 shorter events, 72.9 us)
Async XLA Ops:
  7.2 618.4 %copy-start = (bf16[2880,64]{0,1:T(8,128)(2,1)S(1)}, bf16[2880,64]{0,1:T(8,128)(2,1)}, u32[]{:S(2)}) copy-start(bf16[2880,64]{0,1:T(8,128)(2,1)} %param.22) | copy-start | bytes 1105924
  7.2 357.4 %all-gather.2.cloned.1.call-start = ((), (), s32[]{:S(2)}) async-start(), calls=%async_computation.2 | async-start | bytes 12533760 | tf_op jit(solution)/shard_map/all_gather | solution.py:130
  9.7 19.4 %collective-permute-start = (bf16[384,1024]{0,1:T(8,128)(2,1)S(1)}, bf16[384,1024]{0,1:T(8,128)(2,1)S(1)}, u32[]{:S(2)}, u32[]{:S(2)}) collective-permute-start(bf16[384,1024]{0,1:T(8,128)(2,1)S(1)} %pad_maximum_fusion), channel_id=1, source_target_pairs={{0,8},{8,16},{16,24},{24,32},{32,40},{40,48},{48,56},{56,64},{64,7... | collective-permute-start | bytes 2359304 | tf_op jit(solution)/shard_map/ppermute | solution.py:18
  29.1 20.8 %collective-permute-start.1 = (bf16[384,1024]{0,1:T(8,128)(2,1)S(1)}, bf16[384,1024]{0,1:T(8,128)(2,1)S(1)}, u32[]{:S(2)}, u32[]{:S(2)}) collective-permute-start(bf16[384,1024]{0,1:T(8,128)(2,1)S(1)} %collective-permute-done), channel_id=1, source_target_pairs={{0,8},{8,16},{16,24},{24,32},{32,40},{40,48},{48,56},{56,64},{64,7... | collective-permute-start | bytes 2359304 | tf_op jit(solution)/shard_map/ppermute | solution.py:18
  30.6 19.4 %collective-permute-start.8 = (bf16[384,1024]{0,1:T(8,128)(2,1)S(1)}, bf16[384,1024]{0,1:T(8,128)(2,1)S(1)}, u32[]{:S(2)}, u32[]{:S(2)}) collective-permute-start(bf16[384,1024]{0,1:T(8,128)(2,1)S(1)} %pad_maximum_fusion), channel_id=1, source_target_pairs={{0,120},{8,0},{16,8},{24,16},{32,24},{40,32},{48,40},{56,48},{64,5... | collective-permute-start | bytes 2359304 | tf_op jit(solution)/shard_map/ppermute | solution.py:21
  49.9 21.0 %copy-start.1 = (bf16[384,1024]{0,1:T(8,128)(2,1)}, bf16[384,1024]{0,1:T(8,128)(2,1)S(1)}, u32[]{:S(2)}) copy-start(bf16[384,1024]{0,1:T(8,128)(2,1)S(1)} %collective-permute-done.1) | copy-start | bytes 2359300
  49.9 21.0 %collective-permute-start.2 = (bf16[384,1024]{0,1:T(8,128)(2,1)S(1)}, bf16[384,1024]{0,1:T(8,128)(2,1)S(1)}, u32[]{:S(2)}, u32[]{:S(2)}) collective-permute-start(bf16[384,1024]{0,1:T(8,128)(2,1)S(1)} %collective-permute-done.1), channel_id=1, source_target_pairs={{0,8},{8,16},{16,24},{24,32},{32,40},{40,48},{48,56},{56,64},{64,7... | collective-permute-start | bytes 2359304 | tf_op jit(solution)/shard_map/ppermute | solution.py:18
  49.9 21.0 %collective-permute-start.9 = (bf16[384,1024]{0,1:T(8,128)(2,1)S(1)}, bf16[384,1024]{0,1:T(8,128)(2,1)S(1)}, u32[]{:S(2)}, u32[]{:S(2)}) collective-permute-start(bf16[384,1024]{0,1:T(8,128)(2,1)S(1)} %collective-permute-done.8), channel_id=1, source_target_pairs={{0,120},{8,0},{16,8},{24,16},{32,24},{40,32},{48,40},{56,48},{64,5... | collective-permute-start | bytes 2359304 | tf_op jit(solution)/shard_map/ppermute | solution.py:21
  70.9 20.1 %copy-start.5 = (bf16[384,1024]{0,1:T(8,128)(2,1)}, bf16[384,1024]{0,1:T(8,128)(2,1)S(1)}, u32[]{:S(2)}) copy-start(bf16[384,1024]{0,1:T(8,128)(2,1)S(1)} %collective-permute-done.2) | copy-start | bytes 2359300
  70.9 20.1 %collective-permute-start.3 = (bf16[384,1024]{0,1:T(8,128)(2,1)S(1)}, bf16[384,1024]{0,1:T(8,128)(2,1)S(1)}, u32[]{:S(2)}, u32[]{:S(2)}) collective-permute-start(bf16[384,1024]{0,1:T(8,128)(2,1)S(1)} %collective-permute-done.2), channel_id=1, source_target_pairs={{0,8},{8,16},{16,24},{24,32},{32,40},{40,48},{48,56},{56,64},{64,7... | collective-permute-start | bytes 2359304 | tf_op jit(solution)/shard_map/ppermute | solution.py:18
  70.9 5.1 copy-start.3
  70.9 20.0 %collective-permute-start.10 = (bf16[384,1024]{0,1:T(8,128)(2,1)S(1)}, bf16[384,1024]{0,1:T(8,128)(2,1)S(1)}, u32[]{:S(2)}, u32[]{:S(2)}) collective-permute-start(bf16[384,1024]{0,1:T(8,128)(2,1)S(1)} %collective-permute-done.9), channel_id=1, source_target_pairs={{0,120},{8,0},{16,8},{24,16},{32,24},{40,32},{48,40},{56,48},{64,5... | collective-permute-start | bytes 2359304 | tf_op jit(solution)/shard_map/ppermute | solution.py:21
  91.0 19.2 %copy-start.9 = (bf16[384,1024]{0,1:T(8,128)(2,1)}, bf16[384,1024]{0,1:T(8,128)(2,1)S(1)}, u32[]{:S(2)}) copy-start(bf16[384,1024]{0,1:T(8,128)(2,1)S(1)} %collective-permute-done.3) | copy-start | bytes 2359300
  91.0 19.1 %collective-permute-start.4 = (bf16[384,1024]{0,1:T(8,128)(2,1)S(1)}, bf16[384,1024]{0,1:T(8,128)(2,1)S(1)}, u32[]{:S(2)}, u32[]{:S(2)}) collective-permute-start(bf16[384,1024]{0,1:T(8,128)(2,1)S(1)} %collective-permute-done.3), channel_id=1, source_target_pairs={{0,8},{8,16},{16,24},{24,32},{32,40},{40,48},{48,56},{56,64},{64,7... | collective-permute-start | bytes 2359304 | tf_op jit(solution)/shard_map/ppermute | solution.py:18
  91.0 5.1 copy-start.7
  91.0 19.1 %collective-permute-start.11 = (bf16[384,1024]{0,1:T(8,128)(2,1)S(1)}, bf16[384,1024]{0,1:T(8,128)(2,1)}, u32[]{:S(2)}, u32[]{:S(2)}) collective-permute-start(bf16[384,1024]{0,1:T(8,128)(2,1)S(1)} %collective-permute-done.10), channel_id=1, source_target_pairs={{0,120},{8,0},{16,8},{24,16},{32,24},{40,32},{48,40},{56,48},{64,5... | collective-permute-start | bytes 2359304 | tf_op jit(solution)/shard_map/ppermute | solution.py:21
  110.1 5.2 copy-start.11
  110.1 18.3 %collective-permute-start.5 = (bf16[384,1024]{0,1:T(8,128)(2,1)S(1)}, bf16[384,1024]{0,1:T(8,128)(2,1)}, u32[]{:S(2)}, u32[]{:S(2)}) collective-permute-start(bf16[384,1024]{0,1:T(8,128)(2,1)S(1)} %collective-permute-done.4), channel_id=1, source_target_pairs={{0,8},{8,16},{16,24},{24,32},{32,40},{40,48},{48,56},{56,64},{64,7... | collective-permute-start | bytes 2359304 | tf_op jit(solution)/shard_map/ppermute | solution.py:18
  110.1 25.6 %collective-permute-start.12 = (bf16[384,1024]{0,1:T(8,128)(2,1)}, bf16[384,1024]{0,1:T(8,128)(2,1)}, u32[]{:S(2)}, u32[]{:S(2)}) collective-permute-start(bf16[384,1024]{0,1:T(8,128)(2,1)} %collective-permute-done.11), channel_id=1, source_target_pairs={{0,120},{8,0},{16,8},{24,16},{32,24},{40,32},{48,40},{56,48},{64,5... | collective-permute-start | bytes 2359304 | tf_op jit(solution)/shard_map/ppermute | solution.py:21
  128.4 17.7 %collective-permute-start.6 = (bf16[384,1024]{0,1:T(8,128)(2,1)}, bf16[384,1024]{0,1:T(8,128)(2,1)}, u32[]{:S(2)}, u32[]{:S(2)}) collective-permute-start(bf16[384,1024]{0,1:T(8,128)(2,1)} %collective-permute-done.5), channel_id=1, source_target_pairs={{0,8},{8,16},{16,24},{24,32},{32,40},{40,48},{48,56},{56,64},{64,7... | collective-permute-start | bytes 2359304 | tf_op jit(solution)/shard_map/ppermute | solution.py:18
  135.6 49.4 %copy-start.8 = (bf16[384,1024]{0,1:T(8,128)(2,1)S(1)}, bf16[384,1024]{0,1:T(8,128)(2,1)}, u32[]{:S(2)}) copy-start(bf16[384,1024]{0,1:T(8,128)(2,1)} %copy-done.7) | copy-start | bytes 2359300
  135.7 55.8 %copy-start.12 = (bf16[384,1024]{0,1:T(8,128)(2,1)S(1)}, bf16[384,1024]{0,1:T(8,128)(2,1)}, u32[]{:S(2)}) copy-start(bf16[384,1024]{0,1:T(8,128)(2,1)} %copy-done.11) | copy-start | bytes 2359300
  135.7 56.0 %copy-start.10 = (bf16[384,1024]{0,1:T(8,128)(2,1)S(1)}, bf16[384,1024]{0,1:T(8,128)(2,1)}, u32[]{:S(2)}) copy-start(bf16[384,1024]{0,1:T(8,128)(2,1)} %copy-done.9) | copy-start | bytes 2359300
  135.7 56.2 %copy-start.6 = (bf16[384,1024]{0,1:T(8,128)(2,1)S(1)}, bf16[384,1024]{0,1:T(8,128)(2,1)}, u32[]{:S(2)}) copy-start(bf16[384,1024]{0,1:T(8,128)(2,1)} %copy-done.5) | copy-start | bytes 2359300
  135.7 23.1 %collective-permute-start.13 = (bf16[384,1024]{0,1:T(8,128)(2,1)}, bf16[384,1024]{0,1:T(8,128)(2,1)S(1)}, u32[]{:S(2)}, u32[]{:S(2)}) collective-permute-start(bf16[384,1024]{0,1:T(8,128)(2,1)} %collective-permute-done.12), channel_id=1, source_target_pairs={{0,120},{8,0},{16,8},{24,16},{32,24},{40,32},{48,40},{56,48},{64,5... | collective-permute-start | bytes 2359304 | tf_op jit(solution)/shard_map/ppermute | solution.py:21
  146.1 28.5 %collective-permute-start.7 = (bf16[384,1024]{0,1:T(8,128)(2,1)}, bf16[384,1024]{0,1:T(8,128)(2,1)S(1)}, u32[]{:S(2)}, u32[]{:S(2)}) collective-permute-start(bf16[384,1024]{0,1:T(8,128)(2,1)} %collective-permute-done.6), channel_id=1, source_target_pairs={{0,8},{8,16},{16,24},{24,32},{32,40},{40,48},{48,56},{56,64},{64,7... | collective-permute-start | bytes 2359304 | tf_op jit(solution)/shard_map/ppermute | solution.py:18
  158.7 29.5 %collective-permute-start.14 = (bf16[384,1024]{0,1:T(8,128)(2,1)S(1)}, bf16[384,1024]{0,1:T(8,128)(2,1)S(1)}, u32[]{:S(2)}, u32[]{:S(2)}) collective-permute-start(bf16[384,1024]{0,1:T(8,128)(2,1)S(1)} %collective-permute-done.13), channel_id=1, source_target_pairs={{0,120},{8,0},{16,8},{24,16},{32,24},{40,32},{48,40},{56,48},{64,5... | collective-permute-start | bytes 2359304 | tf_op jit(solution)/shard_map/ppermute | solution.py:21
  174.8 17.4 %copy-start.2 = (bf16[384,1024]{0,1:T(8,128)(2,1)S(1)}, bf16[384,1024]{0,1:T(8,128)(2,1)}, u32[]{:S(2)}) copy-start(bf16[384,1024]{0,1:T(8,128)(2,1)} %copy-done.1) | copy-start | bytes 2359300
  180.3 12.7 %copy-start.4 = (bf16[384,1024]{0,1:T(8,128)(2,1)S(1)}, bf16[384,1024]{0,1:T(8,128)(2,1)}, u32[]{:S(2)}) copy-start(bf16[384,1024]{0,1:T(8,128)(2,1)} %copy-done.3) | copy-start | bytes 2359300
  193.2 14.6 %copy-start.14 = (f32[8,4,128,64]{2,3,1,0:T(8,128)S(1)}, f32[8,4,128,64]{2,3,1,0:T(8,128)}, u32[]{:S(2)}) copy-start(f32[8,4,128,64]{2,3,1,0:T(8,128)} %custom-call.1) | copy-start | bytes 3145732
  364.3 8.9 %copy-start.16 = (f32[2880]{0:T(1024)S(1)}, f32[2880]{0:T(1024)}, u32[]{:S(2)}) copy-start(f32[2880]{0:T(1024)} %param.21) | copy-start | bytes 34564
  372.3 0.9 copy-start.13
  613.4 12.4 %copy-start.15 = (s32[1,128,4]{1,2,0:T(4,128)S(1)}, s32[1,128,4]{1,2,0:T(4,128)}, u32[]{:S(2)}) copy-start(s32[1,128,4]{1,2,0:T(4,128)} %param.23) | copy-start | bytes 6148
  613.4 170.3 %all-to-all-start.1 = ((bf16[128,10,2880]{2,1,0:T(8,128)(2,1)}), bf16[128,10,2880]{2,1,0:T(8,128)(2,1)}, u32[]{:S(2)}, u32[]{:S(2)}) async-start(bf16[128,10,2880]{2,1,0:T(8,128)(2,1)} %reshape.321), calls=%async_computation.1 | async-start | bytes 24117248 | tf_op jit(solution)/shard_map/all_to_all | solution.py:171
Sparse Core Ops, SparseCore 0:
  128.6 123.5 all-gather.1
